TPU v7x, 32 devices: a whole 2x2x4 slice. The times are simulated.
32 devices in a mesh: row: 16 (over z, x, core), col: 2 (over y).
Axes of the slice: x: 2, y: 2, z: 4, core: 2. Of those that a mesh axis runs over, the one named last changes fastest.
Arguments:
- slab: float32 [8192, 1024], P('row', 'col'), may hold values from -6 to 6
- leaf_v: float32 [8192, 256], P('row', 'col'), may hold values from -0.25 to 0.25
- leaf_t: float32 [4096, 256], P('row', 'col'), may hold values from -0.1875 to 0.1875
- tree_v: float32 [4096, 256], P('row', 'col'), may hold values from -0.375 to 0.375
- tree_t: float32 [4096, 256], P('row', 'col'), may hold values from -0.1875 to 0.1875
Outputs:
- updated_slab: float32 [8192, 1024], P('row', 'col')
All inputs are finite; a program needn't handle non-finite values.
Results may differ from a plain program's by a relative error of at most 0.0001.
Values sent between devices are 32-bit elements; how exact they have to be, the bound alone decides.
No kernel may reach another device: no remote copies, remote signals or barrier semaphores. Data moves between devices by JAX's collectives and lax.ppermute only.
A program may use at most 64 MiB of HBM per device.

v0:
```python
import jax
import jax.numpy as jnp
from jax import lax
from jax.sharding import PartitionSpec as P


def swapped(array, axis, bit):
    return lax.ppermute(array, axis, [(i, i ^ 1 << bit) for i in range(lax.axis_size(axis))])


def product(left, right):
    return jnp.dot(left, right, precision=lax.Precision.HIGHEST, preferred_element_type=jnp.float32)


def product_left_t(left, right):
    return lax.dot_general(
        left,
        right,
        (((0,), (0,)), ((), ())),
        precision=lax.Precision.HIGHEST,
        preferred_element_type=jnp.float32,
    )


def unit_lower(raw):
    row_ids = lax.broadcasted_iota(jnp.int32, raw.shape, 0)
    col_ids = lax.broadcasted_iota(jnp.int32, raw.shape, 1)
    diagonal = jnp.where(row_ids == col_ids, 1.0, 0.0).astype(raw.dtype)
    return jnp.where(row_ids > col_ids, raw, 0.0) + diagonal


def on_device(slab, leaf_v, leaf_t, tree_v, tree_t):
    leaf_full, leaf_tri = (
        lax.all_gather(leaf_v, "col", axis=1, tiled=True),
        lax.all_gather(leaf_t, "col", axis=1, tiled=True),
    )
    tree_full, tree_tri = (
        lax.all_gather(tree_v, "col", axis=1, tiled=True),
        lax.all_gather(tree_t, "col", axis=1, tiled=True),
    )
    width = leaf_tri.shape[0]
    leaf_vectors = unit_lower(leaf_full)
    leaf_factor = jnp.triu(leaf_tri)
    leaf_w = product_left_t(leaf_factor, product_left_t(leaf_vectors, slab))
    current = slab[:width] - product(leaf_vectors[:width], leaf_w)
    remainder = slab[width:] - product(leaf_vectors[width:], leaf_w)
    tree_vectors = jnp.triu(tree_full)
    tree_factor = jnp.triu(tree_tri)
    position = lax.axis_index("row")
    levels = lax.axis_size("row").bit_length() - 1
    for level in range(levels):
        step = 1 << level
        phase = position % (2 * step)
        is_lower = phase == 0
        is_upper = phase == step
        projected = product_left_t(tree_vectors, current)
        outgoing = jnp.where(is_upper, projected, current)
        received, partner_factor = swapped((outgoing, tree_factor), "row", level)
        merged = jnp.where(is_upper, received + projected, current + received)
        pair_factor = jnp.where(is_upper, tree_factor, partner_factor)
        update = product_left_t(pair_factor, merged)
        raised = current - product(tree_vectors, update)
        lowered = current - update
        current = jnp.where(is_upper, raised, jnp.where(is_lower, lowered, current))
    return jnp.concatenate([current, remainder], axis=0)


def solution(mesh):
    in_specs = (P("row", "col"), P("row", "col"), P("row", "col"), P("row", "col"), P("row", "col"))
    out_specs = P("row", "col")
    return jax.shard_map(
        on_device, mesh=mesh, in_specs=in_specs, out_specs=out_specs, check_vma=False
    )
```

profile of v0, /device:TPU:0, one launch (start us, length us, event | category | flops | bytes accessed | tf_op | source)
XLA Modules:
  0.0 124.4 jit_solution(8653530077791594265)
XLA Ops:
  0.0 10.3 %all_gather.12 = f32[512,256]{1,0:T(8,128)S(1)} all-gather(f32[512,128]{1,0:T(8,128)} %param.6), channel_id=1, replica_groups=mesh['row'=16,'col'=2] {'col'}, dimensions={1}, use_global_device_ids=true | all-gather | bytes 786432 | tf_op jit(solution)/shard_map/all_gather | solution.py:34
  10.4 1.1 fusion.41
  11.5 5.8 %all_gather.13 = f32[256,256]{1,0:T(8,128)S(1)} all-gather(f32[256,128]{1,0:T(8,128)S(1)} %copy-done.4), channel_id=1, replica_groups=mesh['row'=16,'col'=2] {'col'}, dimensions={1}, use_global_device_ids=true | all-gather | bytes 393216 | tf_op jit(solution)/shard_map/all_gather | solution.py:35
  17.3 5.6 %all_gather.14 = f32[256,256]{1,0:T(8,128)S(1)} all-gather(f32[256,128]{1,0:T(8,128)S(1)} %copy-done.5), channel_id=1, replica_groups=mesh['row'=16,'col'=2] {'col'}, dimensions={1}, use_global_device_ids=true | all-gather | bytes 393216 | tf_op jit(solution)/shard_map/all_gather | solution.py:38
  22.9 0.7 fusion.26
  24.3 1.5 %broadcast_select_fusion = (f32[256,512]{1,0:T(8,128)}, f32[256,512]{1,0:T(8,128)S(1)}) fusion(f32[256,512]{1,0:T(8,128)S(1)} %convolution_subtract_fusion.5, pred[]{:T(512)S(6)} %eq.35, f32[256,256]{1,0:T(8,128)S(1)} %all_gather.14, s32[256]{0:T(256)S(1)} %iota_add_fusion), kind=kOutput, calls=%fused_computation.46 | convolution fusion | flops 402915328 | bytes 1836033 | tf_op jit(solution)/shard_map/dot_general | solution.py:16
  25.8 6.8 %all_gather.15 = f32[256,256]{1,0:T(8,128)S(1)} all-gather(f32[256,128]{1,0:T(8,128)S(1)} %copy-done.6), channel_id=1, replica_groups=mesh['row'=16,'col'=2] {'col'}, dimensions={1}, use_global_device_ids=true | all-gather | bytes 393216 | tf_op jit(solution)/shard_map/all_gather | solution.py:39
  32.7 1.5 %collective-permute-done = f32[256,256]{1,0:T(8,128)S(1)} collective-permute-done((f32[256,256]{1,0:T(8,128)S(1)}, f32[256,256]{1,0:T(8,128)S(1)}, u32[]{:S(2)}, u32[]{:S(2)}) %collective-permute-start) | collective-permute-done | bytes 262176 | tf_op jit(solution)/shard_map/ppermute | solution.py:8
  34.2 1.7 %fusion.16 = f32[256,512]{1,0:T(8,128)S(1)} fusion(f32[256,512]{1,0:T(8,128)S(1)} %convolution_subtract_fusion.5, f32[256,512]{1,0:T(8,128)} %collective-permute-done.1, f32[256,512]{1,0:T(8,128)S(1)} %get-tuple-element.6, f32[256,256]{1,0:T(8,128)S(1)} %fusion.28, f32[256,256]{1,0:T(8,128)S(1)} %collective-permute-done, pred[]{:T(512)S(6)} %eq.35), kind=kOutput, calls=%fused_computation.27 | convolution fusion | flops 403111936 | bytes 2621441 | tf_op jit(solution)/shard_map/dot_general | solution.py:16
  36.7 1.5 %broadcast_select_fusion.1 = (f32[256,512]{1,0:T(8,128)}, f32[256,512]{1,0:T(8,128)S(1)}) fusion(f32[256,512]{1,0:T(8,128)S(1)} %fusion, pred[]{:T(512)S(6)} %eq.34, f32[256,256]{1,0:T(8,128)S(1)} %all_gather.14, s32[256]{0:T(256)S(1)} %iota_add_fusion), kind=kOutput, calls=%fused_computation.48 | convolution fusion | flops 402915328 | bytes 1836033 | tf_op jit(solution)/shard_map/dot_general | solution.py:16
  38.2 1.7 %collective-permute-start.3 = (f32[256,512]{1,0:T(8,128)}, f32[256,512]{1,0:T(8,128)}, u32[]{:S(2)}, u32[]{:S(2)}) collective-permute-start(f32[256,512]{1,0:T(8,128)} %get-tuple-element.7), channel_id=1, source_target_pairs={{0,4},{2,6},{4,0},{6,2},{8,12},{10,14},{12,8},{14,10},{16,20},{18,... | collective-permute-start | bytes 1572872 | tf_op jit(solution)/shard_map/ppermute | solution.py:8
  40.2 17.8 %collective-permute-done.2 = f32[256,256]{1,0:T(8,128)S(1)} collective-permute-done((f32[256,256]{1,0:T(8,128)S(1)}, f32[256,256]{1,0:T(8,128)S(1)}, u32[]{:S(2)}, u32[]{:S(2)}) %collective-permute-start.2) | collective-permute-done | bytes 262176 | tf_op jit(solution)/shard_map/ppermute | solution.py:8
  58.0 1.7 %fusion.12 = f32[256,512]{1,0:T(8,128)S(1)} fusion(f32[256,512]{1,0:T(8,128)S(1)} %fusion, f32[256,512]{1,0:T(8,128)} %collective-permute-done.3, f32[256,512]{1,0:T(8,128)S(1)} %get-tuple-element.8, f32[256,256]{1,0:T(8,128)S(1)} %fusion.28, f32[256,256]{1,0:T(8,128)S(1)} %collective-permute-done.2, pred[]{:T(512)S(6)} %eq.34), kind=kOutput, calls=%fused_computation.23 | convolution fusion | flops 403111936 | bytes 2621441 | tf_op jit(solution)/shard_map/dot_general | solution.py:16
  60.4 1.5 %broadcast_select_fusion.2 = (f32[256,512]{1,0:T(8,128)}, f32[256,512]{1,0:T(8,128)S(1)}) fusion(f32[256,512]{1,0:T(8,128)S(1)} %fusion.1, pred[]{:T(512)S(6)} %eq.33, f32[256,256]{1,0:T(8,128)S(1)} %all_gather.14, s32[256]{0:T(256)S(1)} %iota_add_fusion), kind=kOutput, calls=%fused_computation.50 | convolution fusion | flops 402915328 | bytes 1836033 | tf_op jit(solution)/shard_map/dot_general | solution.py:16
  61.9 1.8 %collective-permute-start.5 = (f32[256,512]{1,0:T(8,128)}, f32[256,512]{1,0:T(8,128)}, u32[]{:S(2)}, u32[]{:S(2)}) collective-permute-start(f32[256,512]{1,0:T(8,128)} %get-tuple-element.9), channel_id=1, source_target_pairs={{0,8},{2,10},{4,12},{6,14},{8,0},{10,2},{12,4},{14,6},{16,24},{18,... | collective-permute-start | bytes 1572872 | tf_op jit(solution)/shard_map/ppermute | solution.py:8
  63.9 17.0 %collective-permute-done.4 = f32[256,256]{1,0:T(8,128)S(1)} collective-permute-done((f32[256,256]{1,0:T(8,128)S(1)}, f32[256,256]{1,0:T(8,128)S(1)}, u32[]{:S(2)}, u32[]{:S(2)}) %collective-permute-start.4) | collective-permute-done | bytes 262176 | tf_op jit(solution)/shard_map/ppermute | solution.py:8
  80.9 1.7 %fusion.8 = f32[256,512]{1,0:T(8,128)S(1)} fusion(f32[256,512]{1,0:T(8,128)S(1)} %fusion.1, f32[256,512]{1,0:T(8,128)} %collective-permute-done.5, f32[256,512]{1,0:T(8,128)S(1)} %get-tuple-element.10, f32[256,256]{1,0:T(8,128)S(1)} %fusion.28, f32[256,256]{1,0:T(8,128)S(1)} %collective-permute-done.4, pred[]{:T(512)S(6)} %eq.33), kind=kOutput, calls=%fused_computation.19 | convolution fusion | flops 403111936 | bytes 2621441 | tf_op jit(solution)/shard_map/dot_general | solution.py:16
  82.6 0.7 fusion.2
  83.3 1.7 %broadcast_select_fusion.3 = (f32[256,512]{1,0:T(8,128)}, f32[256,512]{1,0:T(8,128)}) fusion(f32[256,512]{1,0:T(8,128)S(1)} %fusion.2, pred[]{:T(512)S(6)} %eq.32, f32[256,256]{1,0:T(8,128)S(1)} %all_gather.14, s32[256]{0:T(256)S(1)} %iota_add_fusion), kind=kOutput, calls=%fused_computation.52 | convolution fusion | flops 402915328 | bytes 1836033 | tf_op jit(solution)/shard_map/dot_general | solution.py:16
  85.0 2.8 %collective-permute-start.7 = (f32[256,512]{1,0:T(8,128)}, f32[256,512]{1,0:T(8,128)}, u32[]{:S(2)}, u32[]{:S(2)}) collective-permute-start(f32[256,512]{1,0:T(8,128)} %get-tuple-element.11), channel_id=1, source_target_pairs={{0,16},{2,18},{4,20},{6,22},{8,24},{10,26},{12,28},{14,30},{16,0},... | collective-permute-start | bytes 1572872 | tf_op jit(solution)/shard_map/ppermute | solution.py:8
  88.6 32.4 %collective-permute-done.6 = f32[256,256]{1,0:T(8,128)S(1)} collective-permute-done((f32[256,256]{1,0:T(8,128)S(1)}, f32[256,256]{1,0:T(8,128)S(1)}, u32[]{:S(2)}, u32[]{:S(2)}) %collective-permute-start.6) | collective-permute-done | bytes 262176 | tf_op jit(solution)/shard_map/ppermute | solution.py:8
  120.9 1.7 %fusion.4 = f32[256,512]{1,0:T(8,128)S(1)} fusion(f32[256,512]{1,0:T(8,128)S(1)} %fusion.2, f32[256,512]{1,0:T(8,128)} %collective-permute-done.7, f32[256,512]{1,0:T(8,128)S(1)} %copy-done.3, f32[256,256]{1,0:T(8,128)S(1)} %fusion.28, f32[256,256]{1,0:T(8,128)S(1)} %collective-permute-done.6, pred[]{:T(512)S(6)} %eq.32), kind=kOutput, calls=%fused_computation.15 | convolution fusion | flops 403111936 | bytes 2621441 | tf_op jit(solution)/shard_map/dot_general | solution.py:16
  122.7 0.7 fusion.3
  123.4 1.0 pad_maximum_fusion
  (30 shorter events, 3.6 us)
Async XLA Ops:
  0.0 10.4 %copy-start = (f32[512,512]{1,0:T(8,128)S(1)}, f32[512,512]{1,0:T(8,128)}, u32[]{:S(2)}) copy-start(f32[512,512]{1,0:T(8,128)} %param.5) | copy-start | bytes 3145732
  10.4 13.2 %copy-start.1 = (f32[512,256]{1,0:T(8,128)}, f32[512,256]{1,0:T(8,128)S(1)}, u32[]{:S(2)}) copy-start(f32[512,256]{1,0:T(8,128)S(1)} %select_add_fusion) | copy-start | bytes 1572868
  10.4 1.1 copy-start.4
  11.5 5.8 %copy-start.5 = (f32[256,128]{1,0:T(8,128)S(1)}, f32[256,128]{1,0:T(8,128)}, u32[]{:S(2)}) copy-start(f32[256,128]{1,0:T(8,128)} %param.8) | copy-start | bytes 393220
  24.3 1.5 %copy-start.6 = (f32[256,128]{1,0:T(8,128)S(1)}, f32[256,128]{1,0:T(8,128)}, u32[]{:S(2)}) copy-start(f32[256,128]{1,0:T(8,128)} %param.9) | copy-start | bytes 393220
  25.8 8.5 %collective-permute-start.1 = (f32[256,512]{1,0:T(8,128)}, f32[256,512]{1,0:T(8,128)}, u32[]{:S(2)}, u32[]{:S(2)}) collective-permute-start(f32[256,512]{1,0:T(8,128)} %get-tuple-element.5), channel_id=1, source_target_pairs={{0,2},{2,0},{4,6},{6,4},{8,10},{10,8},{12,14},{14,12},{16,18},{18,... | collective-permute-start | bytes 1572872 | tf_op jit(solution)/shard_map/ppermute | solution.py:8
  32.6 1.6 %collective-permute-start = (f32[256,256]{1,0:T(8,128)S(1)}, f32[256,256]{1,0:T(8,128)S(1)}, u32[]{:S(2)}, u32[]{:S(2)}) collective-permute-start(f32[256,256]{1,0:T(8,128)S(1)} %fusion.28), channel_id=1, source_target_pairs={{0,2},{2,0},{4,6},{6,4},{8,10},{10,8},{12,14},{14,12},{16,18},{18,... | collective-permute-start | bytes 786440 | tf_op jit(solution)/shard_map/ppermute | solution.py:8
  38.2 19.8 %collective-permute-start.3 = (f32[256,512]{1,0:T(8,128)}, f32[256,512]{1,0:T(8,128)}, u32[]{:S(2)}, u32[]{:S(2)}) collective-permute-start(f32[256,512]{1,0:T(8,128)} %get-tuple-element.7), channel_id=1, source_target_pairs={{0,4},{2,6},{4,0},{6,2},{8,12},{10,14},{12,8},{14,10},{16,20},{18,... | collective-permute-start | bytes 1572872 | tf_op jit(solution)/shard_map/ppermute | solution.py:8
  39.8 18.1 %collective-permute-start.2 = (f32[256,256]{1,0:T(8,128)S(1)}, f32[256,256]{1,0:T(8,128)S(1)}, u32[]{:S(2)}, u32[]{:S(2)}) collective-permute-start(f32[256,256]{1,0:T(8,128)S(1)} %fusion.28), channel_id=1, source_target_pairs={{0,4},{2,6},{4,0},{6,2},{8,12},{10,14},{12,8},{14,10},{16,20},{18,... | collective-permute-start | bytes 786440 | tf_op jit(solution)/shard_map/ppermute | solution.py:8
  61.9 19.0 %collective-permute-start.5 = (f32[256,512]{1,0:T(8,128)}, f32[256,512]{1,0:T(8,128)}, u32[]{:S(2)}, u32[]{:S(2)}) collective-permute-start(f32[256,512]{1,0:T(8,128)} %get-tuple-element.9), channel_id=1, source_target_pairs={{0,8},{2,10},{4,12},{6,14},{8,0},{10,2},{12,4},{14,6},{16,24},{18,... | collective-permute-start | bytes 1572872 | tf_op jit(solution)/shard_map/ppermute | solution.py:8
  63.7 17.2 %collective-permute-start.4 = (f32[256,256]{1,0:T(8,128)S(1)}, f32[256,256]{1,0:T(8,128)S(1)}, u32[]{:S(2)}, u32[]{:S(2)}) collective-permute-start(f32[256,256]{1,0:T(8,128)S(1)} %fusion.28), channel_id=1, source_target_pairs={{0,8},{2,10},{4,12},{6,14},{8,0},{10,2},{12,4},{14,6},{16,24},{18,... | collective-permute-start | bytes 786440 | tf_op jit(solution)/shard_map/ppermute | solution.py:8
  83.3 4.6 %copy-start.2 = (f32[512,256]{1,0:T(8,128)S(1)}, f32[512,256]{1,0:T(8,128)}, u32[]{:S(2)}) copy-start(f32[512,256]{1,0:T(8,128)} %copy-done.1) | copy-start | bytes 1572868
  85.0 35.9 %collective-permute-start.7 = (f32[256,512]{1,0:T(8,128)}, f32[256,512]{1,0:T(8,128)}, u32[]{:S(2)}, u32[]{:S(2)}) collective-permute-start(f32[256,512]{1,0:T(8,128)} %get-tuple-element.11), channel_id=1, source_target_pairs={{0,16},{2,18},{4,20},{6,22},{8,24},{10,26},{12,28},{14,30},{16,0},... | collective-permute-start | bytes 1572872 | tf_op jit(solution)/shard_map/ppermute | solution.py:8
  87.8 33.2 %collective-permute-start.6 = (f32[256,256]{1,0:T(8,128)S(1)}, f32[256,256]{1,0:T(8,128)S(1)}, u32[]{:S(2)}, u32[]{:S(2)}) collective-permute-start(f32[256,256]{1,0:T(8,128)S(1)} %fusion.28), channel_id=1, source_target_pairs={{0,16},{2,18},{4,20},{6,22},{8,24},{10,26},{12,28},{14,30},{16,0},... | collective-permute-start | bytes 786440 | tf_op jit(solution)/shard_map/ppermute | solution.py:8
  87.9 33.0 %copy-start.3 = (f32[256,512]{1,0:T(8,128)S(1)}, f32[256,512]{1,0:T(8,128)}, u32[]{:S(2)}) copy-start(f32[256,512]{1,0:T(8,128)} %get-tuple-element.12) | copy-start | bytes 1572868
where the time goes:
time: 125 us; the launch traced here: 124 us
  waiting for transfers between devices  68.6 us (55%)
  blocking collectives  28.5 us (23%)
  matrix products  18.8 us (15%)
  starting transfers between devices  7.05 us (6%)
    ppermute x8, waiting for transfers between devices, swapped(): lax.ppermute(array, axis, [(i, i ^ 1 << bit) for i in range(lax.axis_size...  68.6 us
    dot_general x10, matrix products, product_left_t(): lax.dot_general(left, right, (((0,), (0,)), ((), ())), precision=lax.Prec...  14.9 us
    all_gather x1, blocking collectives, on_device(): lax.all_gather(leaf_v, 'col', axis=1, tiled=True)  10.3 us
    ppermute x8, starting transfers between devices, swapped(): lax.ppermute(array, axis, [(i, i ^ 1 << bit) for i in range(lax.axis_size...  7.05 us
    all_gather x1, blocking collectives, on_device(): lax.all_gather(tree_t, 'col', axis=1, tiled=True)  6.75 us
    all_gather x1, blocking collectives, on_device(): lax.all_gather(leaf_t, 'col', axis=1, tiled=True)  5.78 us
    all_gather x1, blocking collectives, on_device(): lax.all_gather(tree_v, 'col', axis=1, tiled=True)  5.63 us
    dot_general x6, matrix products, product(): jnp.dot(left, right, precision=lax.Precision.HIGHEST, preferred_element_t...  3.94 us
  transfers between devices with their start and end apart: 8, of which 4 were waited for; matrix products, arithmetic and copies ran while one was open for 1% of the time, Pallas kernels for 0%

commit v1 on v0

--- a/solution.py
+++ b/solution.py
@@ -2,6 +2,18 @@
 import jax.numpy as jnp
 from jax import lax
 from jax.sharding import PartitionSpec as P
+
+
+def collect(shard, axis, dim):
+    ways, here, turn = (lax.axis_size(axis), lax.axis_index(axis), shard.shape[dim])
+    line, have = (shard, 1)
+    while have < ways:
+        line = jnp.concatenate(
+            [line, lax.ppermute(line, axis, [(d, (d - have) % ways) for d in range(ways)])],
+            axis=dim,
+        )
+        have = 2 * have
+    return jnp.roll(line, here * turn, axis=dim)
 
 
 def swapped(array, axis, bit):
@@ -31,7 +43,7 @@
 
 def on_device(slab, leaf_v, leaf_t, tree_v, tree_t):
     leaf_full, leaf_tri = (
-        lax.all_gather(leaf_v, "col", axis=1, tiled=True),
+        collect(leaf_v, "col", 1),
         lax.all_gather(leaf_t, "col", axis=1, tiled=True),
     )
     tree_full, tree_tri = (

time: 125 us -> 118 us (0.944)
  blocking collectives: 28.5 us -> 21.9 us
  matrix products: 18.8 us -> 15.5 us
  starting transfers between devices: 7.05 us -> 10 us
    all_gather x1 -> x0, blocking collectives: 10.3 us -> none  [on_device(): lax.all_gather(leaf_v, 'col', axis=1, tiled=True)]
    dot_general x10, matrix products: 14.9 us -> 10.5 us  [product_left_t(): lax.dot_general(left, right, (((0,), (0,)), ((), ())), precision=lax.Prec...]
    all_gather x1, blocking collectives: 5.78 us -> 9.32 us  [on_device(): lax.all_gather(leaf_t, 'col', axis=1, tiled=True)]
    ppermute x0 -> x1, starting transfers between devices: none -> 2.97 us  [collect(): lax.ppermute(line, axis, [(d, (d - have) % ways) for d in range(ways)])]
  transfers between devices with their start and end apart: 8 -> 9, of which waited for: 4 -> 4; matrix products, arithmetic and copies ran while one was open for 1% -> 1% of each run, Pallas kernels for 0% -> 0%
where the time goes in v1:
time: 118 us; the launch traced here: 117 us
  waiting for transfers between devices  67.6 us (57%)
  blocking collectives  21.9 us (19%)
  matrix products  15.5 us (13%)
  starting transfers between devices  10 us (8%)
  other arithmetic  2.22 us (2%)
    ppermute x8, waiting for transfers between devices, swapped(): lax.ppermute(array, axis, [(i, i ^ 1 << bit) for i in range(lax.axis_size...  67.6 us
    dot_general x10, matrix products, product_left_t(): lax.dot_general(left, right, (((0,), (0,)), ((), ())), precision=lax.Prec...  10.5 us
    all_gather x1, blocking collectives, on_device(): lax.all_gather(leaf_t, 'col', axis=1, tiled=True)  9.32 us
    ppermute x8, starting transfers between devices, swapped(): lax.ppermute(array, axis, [(i, i ^ 1 << bit) for i in range(lax.axis_size...  7.05 us
    all_gather x1, blocking collectives, on_device(): lax.all_gather(tree_t, 'col', axis=1, tiled=True)  6.75 us
    all_gather x1, blocking collectives, on_device(): lax.all_gather(tree_v, 'col', axis=1, tiled=True)  5.84 us
    dot_general x6, matrix products, product(): jnp.dot(left, right, precision=lax.Precision.HIGHEST, preferred_element_t...  4.98 us
    ppermute x1, starting transfers between devices, collect(): lax.ppermute(line, axis, [(d, (d - have) % ways) for d in range(ways)])  2.97 us
  transfers between devices with their start and end apart: 9, of which 4 were waited for; matrix products, arithmetic and copies ran while one was open for 1% of the time, Pallas kernels for 0%

profile of v1, /device:TPU:0, one launch (start us, length us, event | category | flops | bytes accessed | tf_op | source)
XLA Modules:
  0.0 117.4 jit_solution(7074838370967924762)
XLA Ops:
  0.0 3.0 %collective-permute-start = (f32[512,128]{1,0:T(8,128)}, f32[512,128]{1,0:T(8,128)S(1)}, u32[]{:S(2)}, u32[]{:S(2)}) collective-permute-start(f32[512,128]{1,0:T(8,128)} %param.6), channel_id=1, source_target_pairs={{0,1},{1,0},{2,3},{3,2},{4,5},{5,4},{6,7},{7,6},{8,9},{9,8},{10,11... | collective-permute-start | bytes 786440 | tf_op jit(solution)/shard_map/ppermute | solution.py:12
  3.0 9.3 %all_gather.9 = f32[256,256]{1,0:T(8,128)S(1)} all-gather(f32[256,128]{1,0:T(8,128)} %param.7), channel_id=1, replica_groups=mesh['row'=16,'col'=2] {'col'}, dimensions={1}, use_global_device_ids=true | all-gather | bytes 393216 | tf_op jit(solution)/shard_map/all_gather | solution.py:47
  12.3 5.8 %all_gather.10 = f32[256,256]{1,0:T(8,128)S(1)} all-gather(f32[256,128]{1,0:T(8,128)} %param.8), channel_id=1, replica_groups=mesh['row'=16,'col'=2] {'col'}, dimensions={1}, use_global_device_ids=true | all-gather | bytes 393216 | tf_op jit(solution)/shard_map/all_gather | solution.py:50
  18.1 1.1 fusion.8
  19.2 1.1 fusion.66
  20.3 0.7 fusion.31
  21.6 1.5 %broadcast_select_fusion = (f32[256,512]{1,0:T(8,128)}, f32[256,512]{1,0:T(8,128)S(1)}) fusion(f32[256,512]{1,0:T(8,128)S(1)} %convolution_subtract_fusion.5, pred[]{:T(512)S(6)} %eq.38, f32[256,256]{1,0:T(8,128)S(1)} %all_gather.10, s32[256]{0:T(256)S(1)} %iota_add_fusion), kind=kOutput, calls=%fused_computation.54 | convolution fusion | flops 402915328 | bytes 1836033 | tf_op jit(solution)/shard_map/dot_general | solution.py:28
  23.2 6.8 %all_gather.11 = f32[256,256]{1,0:T(8,128)S(1)} all-gather(f32[256,128]{1,0:T(8,128)S(1)} %copy-done.1), channel_id=1, replica_groups=mesh['row'=16,'col'=2] {'col'}, dimensions={1}, use_global_device_ids=true | all-gather | bytes 393216 | tf_op jit(solution)/shard_map/all_gather | solution.py:51
  30.1 1.5 %collective-permute-done.1 = f32[256,256]{1,0:T(8,128)S(1)} collective-permute-done((f32[256,256]{1,0:T(8,128)S(1)}, f32[256,256]{1,0:T(8,128)S(1)}, u32[]{:S(2)}, u32[]{:S(2)}) %collective-permute-start.1) | collective-permute-done | bytes 262176 | tf_op jit(solution)/shard_map/ppermute | solution.py:20
  31.6 0.7 fusion.21
  33.0 1.5 %broadcast_select_fusion.1 = (f32[256,512]{1,0:T(8,128)}, f32[256,512]{1,0:T(8,128)S(1)}) fusion(f32[256,512]{1,0:T(8,128)S(1)} %fusion, pred[]{:T(512)S(6)} %eq.37, f32[256,256]{1,0:T(8,128)S(1)} %all_gather.10, s32[256]{0:T(256)S(1)} %iota_add_fusion), kind=kOutput, calls=%fused_computation.56 | convolution fusion | flops 402915328 | bytes 1836033 | tf_op jit(solution)/shard_map/dot_general | solution.py:28
  34.5 1.7 %collective-permute-start.4 = (f32[256,512]{1,0:T(8,128)}, f32[256,512]{1,0:T(8,128)S(1)}, u32[]{:S(2)}, u32[]{:S(2)}) collective-permute-start(f32[256,512]{1,0:T(8,128)} %get-tuple-element.7), channel_id=1, source_target_pairs={{0,4},{2,6},{4,0},{6,2},{8,12},{10,14},{12,8},{14,10},{16,20},{18,... | collective-permute-start | bytes 1572872 | tf_op jit(solution)/shard_map/ppermute | solution.py:20
  36.5 17.8 %collective-permute-done.3 = f32[256,256]{1,0:T(8,128)S(1)} collective-permute-done((f32[256,256]{1,0:T(8,128)S(1)}, f32[256,256]{1,0:T(8,128)S(1)}, u32[]{:S(2)}, u32[]{:S(2)}) %collective-permute-start.3) | collective-permute-done | bytes 262176 | tf_op jit(solution)/shard_map/ppermute | solution.py:20
  54.3 0.7 fusion.17
  55.7 1.5 %broadcast_select_fusion.2 = (f32[256,512]{1,0:T(8,128)}, f32[256,512]{1,0:T(8,128)S(1)}) fusion(f32[256,512]{1,0:T(8,128)S(1)} %fusion.1, pred[]{:T(512)S(6)} %eq.36, f32[256,256]{1,0:T(8,128)S(1)} %all_gather.10, s32[256]{0:T(256)S(1)} %iota_add_fusion), kind=kOutput, calls=%fused_computation.58 | convolution fusion | flops 402915328 | bytes 1836033 | tf_op jit(solution)/shard_map/dot_general | solution.py:28
  57.2 1.8 %collective-permute-start.6 = (f32[256,512]{1,0:T(8,128)}, f32[256,512]{1,0:T(8,128)S(1)}, u32[]{:S(2)}, u32[]{:S(2)}) collective-permute-start(f32[256,512]{1,0:T(8,128)} %get-tuple-element.9), channel_id=1, source_target_pairs={{0,8},{2,10},{4,12},{6,14},{8,0},{10,2},{12,4},{14,6},{16,24},{18,... | collective-permute-start | bytes 1572872 | tf_op jit(solution)/shard_map/ppermute | solution.py:20
  59.2 17.0 %collective-permute-done.5 = f32[256,256]{1,0:T(8,128)S(1)} collective-permute-done((f32[256,256]{1,0:T(8,128)S(1)}, f32[256,256]{1,0:T(8,128)S(1)}, u32[]{:S(2)}, u32[]{:S(2)}) %collective-permute-start.5) | collective-permute-done | bytes 262176 | tf_op jit(solution)/shard_map/ppermute | solution.py:20
  76.2 0.7 fusion.13
  77.6 1.5 %broadcast_select_fusion.3 = (f32[256,512]{1,0:T(8,128)}, f32[256,512]{1,0:T(8,128)S(1)}) fusion(f32[256,512]{1,0:T(8,128)S(1)} %fusion.2, pred[]{:T(512)S(6)} %eq.35, f32[256,256]{1,0:T(8,128)S(1)} %all_gather.10, s32[256]{0:T(256)S(1)} %iota_add_fusion), kind=kOutput, calls=%fused_computation.60 | convolution fusion | flops 402915328 | bytes 1836033 | tf_op jit(solution)/shard_map/dot_general | solution.py:28
  79.1 2.8 %collective-permute-start.8 = (f32[256,512]{1,0:T(8,128)}, f32[256,512]{1,0:T(8,128)S(1)}, u32[]{:S(2)}, u32[]{:S(2)}) collective-permute-start(f32[256,512]{1,0:T(8,128)} %get-tuple-element.11), channel_id=1, source_target_pairs={{0,16},{2,18},{4,20},{6,22},{8,24},{10,26},{12,28},{14,30},{16,0},... | collective-permute-start | bytes 1572872 | tf_op jit(solution)/shard_map/ppermute | solution.py:20
  82.0 1.7 %convolution_subtract_fusion = f32[256,512]{1,0:T(8,128)S(1)} fusion(f32[256,512]{1,0:T(8,128)S(1)} %fusion.31, f32[512,512]{1,0:T(8,128)} %param.5, f32[512,256]{1,0:T(8,128)S(1)} %fusion.8), kind=kOutput, calls=%fused_computation | convolution fusion | flops 402784256 | bytes 1835008 | tf_op jit(solution)/shard_map/dot_general | solution.py:24
  83.7 31.3 %collective-permute-done.7 = f32[256,256]{1,0:T(8,128)S(1)} collective-permute-done((f32[256,256]{1,0:T(8,128)S(1)}, f32[256,256]{1,0:T(8,128)S(1)}, u32[]{:S(2)}, u32[]{:S(2)}) %collective-permute-start.7) | collective-permute-done | bytes 262176 | tf_op jit(solution)/shard_map/ppermute | solution.py:20
  115.0 0.7 fusion.9
  116.4 1.0 pad_maximum_fusion
  (21 shorter events, 4.2 us)
Async XLA Ops:
  0.0 19.2 %copy-start = (f32[512,512]{1,0:T(8,128)S(1)}, f32[512,512]{1,0:T(8,128)}, u32[]{:S(2)}) copy-start(f32[512,512]{1,0:T(8,128)} %param.5) | copy-start | bytes 3145732
  0.0 18.1 %collective-permute-start = (f32[512,128]{1,0:T(8,128)}, f32[512,128]{1,0:T(8,128)S(1)}, u32[]{:S(2)}, u32[]{:S(2)}) collective-permute-start(f32[512,128]{1,0:T(8,128)} %param.6), channel_id=1, source_target_pairs={{0,1},{1,0},{2,3},{3,2},{4,5},{5,4},{6,7},{7,6},{8,9},{9,8},{10,11... | collective-permute-start | bytes 786440 | tf_op jit(solution)/shard_map/ppermute | solution.py:12
  21.6 1.5 %copy-start.1 = (f32[256,128]{1,0:T(8,128)S(1)}, f32[256,128]{1,0:T(8,128)}, u32[]{:S(2)}) copy-start(f32[256,128]{1,0:T(8,128)} %param.9) | copy-start | bytes 393220
  23.1 8.5 %collective-permute-start.2 = (f32[256,512]{1,0:T(8,128)}, f32[256,512]{1,0:T(8,128)S(1)}, u32[]{:S(2)}, u32[]{:S(2)}) collective-permute-start(f32[256,512]{1,0:T(8,128)} %get-tuple-element.5), channel_id=1, source_target_pairs={{0,2},{2,0},{4,6},{6,4},{8,10},{10,8},{12,14},{14,12},{16,18},{18,... | collective-permute-start | bytes 1572872 | tf_op jit(solution)/shard_map/ppermute | solution.py:20
  30.0 1.6 %collective-permute-start.1 = (f32[256,256]{1,0:T(8,128)S(1)}, f32[256,256]{1,0:T(8,128)S(1)}, u32[]{:S(2)}, u32[]{:S(2)}) collective-permute-start(f32[256,256]{1,0:T(8,128)S(1)} %fusion.33), channel_id=1, source_target_pairs={{0,2},{2,0},{4,6},{6,4},{8,10},{10,8},{12,14},{14,12},{16,18},{18,... | collective-permute-start | bytes 786440 | tf_op jit(solution)/shard_map/ppermute | solution.py:20
  34.5 19.8 %collective-permute-start.4 = (f32[256,512]{1,0:T(8,128)}, f32[256,512]{1,0:T(8,128)S(1)}, u32[]{:S(2)}, u32[]{:S(2)}) collective-permute-start(f32[256,512]{1,0:T(8,128)} %get-tuple-element.7), channel_id=1, source_target_pairs={{0,4},{2,6},{4,0},{6,2},{8,12},{10,14},{12,8},{14,10},{16,20},{18,... | collective-permute-start | bytes 1572872 | tf_op jit(solution)/shard_map/ppermute | solution.py:20
  36.2 18.1 %collective-permute-start.3 = (f32[256,256]{1,0:T(8,128)S(1)}, f32[256,256]{1,0:T(8,128)S(1)}, u32[]{:S(2)}, u32[]{:S(2)}) collective-permute-start(f32[256,256]{1,0:T(8,128)S(1)} %fusion.33), channel_id=1, source_target_pairs={{0,4},{2,6},{4,0},{6,2},{8,12},{10,14},{12,8},{14,10},{16,20},{18,... | collective-permute-start | bytes 786440 | tf_op jit(solution)/shard_map/ppermute | solution.py:20
  57.2 19.0 %collective-permute-start.6 = (f32[256,512]{1,0:T(8,128)}, f32[256,512]{1,0:T(8,128)S(1)}, u32[]{:S(2)}, u32[]{:S(2)}) collective-permute-start(f32[256,512]{1,0:T(8,128)} %get-tuple-element.9), channel_id=1, source_target_pairs={{0,8},{2,10},{4,12},{6,14},{8,0},{10,2},{12,4},{14,6},{16,24},{18,... | collective-permute-start | bytes 1572872 | tf_op jit(solution)/shard_map/ppermute | solution.py:20
  59.0 17.2 %collective-permute-start.5 = (f32[256,256]{1,0:T(8,128)S(1)}, f32[256,256]{1,0:T(8,128)S(1)}, u32[]{:S(2)}, u32[]{:S(2)}) collective-permute-start(f32[256,256]{1,0:T(8,128)S(1)} %fusion.33), channel_id=1, source_target_pairs={{0,8},{2,10},{4,12},{6,14},{8,0},{10,2},{12,4},{14,6},{16,24},{18,... | collective-permute-start | bytes 786440 | tf_op jit(solution)/shard_map/ppermute | solution.py:20
  79.1 35.9 %collective-permute-start.8 = (f32[256,512]{1,0:T(8,128)}, f32[256,512]{1,0:T(8,128)S(1)}, u32[]{:S(2)}, u32[]{:S(2)}) collective-permute-start(f32[256,512]{1,0:T(8,128)} %get-tuple-element.11), channel_id=1, source_target_pairs={{0,16},{2,18},{4,20},{6,22},{8,24},{10,26},{12,28},{14,30},{16,0},... | collective-permute-start | bytes 1572872 | tf_op jit(solution)/shard_map/ppermute | solution.py:20
  81.8 33.2 %collective-permute-start.7 = (f32[256,256]{1,0:T(8,128)S(1)}, f32[256,256]{1,0:T(8,128)S(1)}, u32[]{:S(2)}, u32[]{:S(2)}) collective-permute-start(f32[256,256]{1,0:T(8,128)S(1)} %fusion.33), channel_id=1, source_target_pairs={{0,16},{2,18},{4,20},{6,22},{8,24},{10,26},{12,28},{14,30},{16,0},... | collective-permute-start | bytes 786440 | tf_op jit(solution)/shard_map/ppermute | solution.py:20
